TPU v7x, 512 devices: a whole 4x8x8 slice. The times are simulated.
512 devices in a mesh: pipe: 32 (over y, z_lo), seq: 16 (over z_hi, x, core).
Axes of the slice: x: 4, y: 8, z: 8 (z_hi: 2, z_lo: 4; z = z_hi * 4 + z_lo), core: 2. Of those that a mesh axis runs over, the one named last changes fastest.
Arguments:
- x_first: bfloat16 [4096, 2560], P(('pipe', 'seq')), may hold values from -6 to 6
- x_second: bfloat16 [4096, 2560], P(('pipe', 'seq')), may hold values from -6 to 6
- stale_kv: bfloat16 [2, 4096, 2048], P(None, 'pipe', 'seq'), may hold values from -6 to 6
- w_qkv: bfloat16 [3, 2560, 2048], P(None, None, 'seq'), may hold values from -0.125 to 0.125
- w_out: bfloat16 [2048, 2560], P('seq'), may hold values from -0.125 to 0.125
- q_gain: float32 [2048], P('seq'), may hold values from 0.4 to 5
- k_gain: float32 [2048], P('seq'), may hold values from 0.4 to 5
- layout: int32 [32, 16], replicated, may hold values from 0 to 31, as said below
- counts: int32 [32], replicated, may hold values from 1 to 16, as said below
- slot_block: int32 [32], replicated, may hold values from 0 to 31, each once
Outputs:
- out_first: bfloat16 [4096, 2560], P(('pipe', 'seq'))
- out_second: bfloat16 [4096, 2560], P(('pipe', 'seq'))
Inputs may be any that keep to these rules, and one draw needn't show every extreme that they name: `layout`: entries of a row are distinct sequence blocks and the first entry of row b is b itself. `counts`: some block reads 16 entries. `slot_block`: each block once.
All inputs are finite; a program needn't handle non-finite values.
Results may differ from a plain program's by a relative error of at most 0.019.
Values may be sent and summed in bfloat16 or wider, within the bound.
No kernel may reach another device: no remote copies, remote signals or barrier semaphores. Data moves between devices by JAX's collectives and lax.ppermute only.
A program may use at most 64 MiB of HBM per device.

v0:
```python
import math
import jax
import jax.numpy as jnp
import numpy as np
from jax import lax
from jax.sharding import Mesh
from jax.sharding import PartitionSpec as P

HS = 64
BLOCK = 128
BPM = 1
HIGH = lax.Precision.HIGHEST
NEG = -1e30
PIPE_PARTS = (("y", 8), ("zl", 4))
SEQ_PARTS = (("zh", 2), ("x", 4), ("c", 2))
PIPE = tuple((n for n, _ in PIPE_PARTS))
SEQ = tuple((n for n, _ in SEQ_PARTS))


def slot_mask(layout, counts, slot_block):
    total = layout.shape[0]
    width = layout.shape[1]
    blocks = jnp.arange(total, dtype=jnp.int32)
    valid = jnp.arange(width, dtype=jnp.int32)[None, :] < counts[:, None]
    member = jnp.sum(
        ((layout[:, :, None] == blocks[None, None, :]) & valid[:, :, None]).astype(jnp.float32),
        axis=1,
    )
    placed = (slot_block[:, None] == blocks[None, :]).astype(jnp.float32)
    linked = jnp.dot(jnp.dot(placed, member, precision=HIGH), placed.T, precision=HIGH)
    return linked > 0.5


def normalize(raw, gain, size):
    count = raw.shape[0]
    grid = raw.reshape(count, -1, size)
    factor = lax.rsqrt(jnp.mean(grid * grid, axis=2, keepdims=True) + 1e-06)
    return (grid * factor).reshape(count, -1) * gain[None, :]


def partial_attend(query, keys, values, allowed, scale):
    heads = query.shape[1]
    qrows = query.shape[0]
    krows = keys.shape[0]
    scores = jnp.einsum("qhd,khd->hqk", query, keys, preferred_element_type=jnp.float32) * scale
    grid = scores.reshape(heads, qrows // BLOCK, BLOCK, krows // BLOCK, BLOCK)
    keep = allowed[None, :, None, :, None]
    grid = jnp.where(keep, grid, NEG)
    top = jnp.max(grid, axis=(3, 4))
    weights = jnp.where(keep, jnp.exp(grid - top[:, :, :, None, None]), 0.0)
    total = jnp.sum(weights, axis=(3, 4))
    weights = weights.reshape(heads, qrows, krows)
    summed = jnp.einsum("hqk,khd->qhd", weights, values.astype(jnp.float32), precision=HIGH)
    return (top.reshape(heads, qrows), total.reshape(heads, qrows), summed)


def merge_parts(first, second):
    top_a, total_a, summed_a = first
    top_b, total_b, summed_b = second
    best = jnp.maximum(top_a, top_b)
    keep_a = jnp.exp(top_a - best)
    keep_b = jnp.exp(top_b - best)
    merged = summed_a * keep_a.T[:, :, None] + summed_b * keep_b.T[:, :, None]
    return (best, total_a * keep_a + total_b * keep_b, merged)


def gather_pipe(piece):
    for name in reversed(PIPE):
        piece = lax.all_gather(piece, name, axis=0, tiled=True)
    return piece


def on_device(
    x_first, x_second, stale_kv, w_qkv, w_out, q_gain, k_gain, layout, counts, slot_block
):
    me = lax.axis_index(PIPE)
    n_seq = math.prod((s for _, s in SEQ_PARTS))
    tokens = BPM * BLOCK
    heads = w_qkv.shape[2] // HS
    width = heads * HS
    scale = 1.0 / math.sqrt(HS)
    linked = slot_mask(layout, counts, slot_block)
    total_blocks = linked.shape[0]
    block_ids = jnp.arange(total_blocks, dtype=jnp.int32)
    batch_of = block_ids // BPM
    mine = lax.dynamic_slice_in_dim(linked, me * BPM, BPM, 0)
    own = lax.dynamic_slice_in_dim(mine, me * BPM, BPM, 1)
    remote = mine & (batch_of != me)[None, :]
    xs = lax.all_gather(jnp.stack([x_first, x_second]), SEQ, axis=1, tiled=True)

    def project(x):
        raw = jnp.einsum("rd,cdh->crh", x, w_qkv, preferred_element_type=jnp.float32)
        query = normalize(raw[0], q_gain, HS).astype(jnp.bfloat16)
        keys = normalize(raw[1], k_gain, HS).astype(jnp.bfloat16)
        values = raw[2].astype(jnp.bfloat16)
        return (query, keys, values)

    q1, k1, v1 = project(xs[0])
    q2, k2, v2 = project(xs[1])
    kv = jnp.stack([stale_kv[0], stale_kv[1], k1, v1])[None]
    gathered = gather_pipe(kv)
    count = gathered.shape[0] * tokens

    def attend(query, keys, values, piece_k, piece_v):
        query_h = query.reshape(tokens, heads, HS)
        start_part = partial_attend(
            query_h, keys.reshape(tokens, heads, HS), values.reshape(tokens, heads, HS), own, scale
        )
        fresh = partial_attend(
            query_h,
            piece_k.reshape(count, heads, HS),
            piece_v.reshape(count, heads, HS),
            remote,
            scale,
        )
        best, denom_h, numer = merge_parts(start_part, fresh)
        denom = denom_h.T
        attn = (numer / denom[:, :, None]).reshape(tokens, width).astype(jnp.bfloat16)
        return jnp.dot(attn, w_out, preferred_element_type=jnp.float32).astype(jnp.bfloat16)

    part1 = attend(q1, k1, v1, gathered[:, 0], gathered[:, 1])
    part2 = attend(q2, k2, v2, gathered[:, 2], gathered[:, 3])
    parts = jnp.stack([part1, part2])
    sent = lax.all_to_all(parts.reshape(2, n_seq, tokens // n_seq, -1), SEQ, 1, 1, tiled=False)
    out = jnp.sum(sent.astype(jnp.float32), axis=1).astype(jnp.bfloat16)
    return (out[0], out[1])


def solution(mesh):
    names = PIPE_PARTS + SEQ_PARTS
    fine = Mesh(
        np.asarray(mesh.devices).reshape([s for _, s in names]), tuple((n for n, _ in names))
    )
    rows = P(PIPE + SEQ, None)
    placed = (
        rows,
        rows,
        P(None, PIPE, SEQ),
        P(None, None, SEQ),
        P(SEQ, None),
        P(SEQ),
        P(SEQ),
        P(),
        P(),
        P(),
    )
    return jax.shard_map(
        on_device, mesh=fine, in_specs=placed, out_specs=(rows, rows), check_vma=False
    )
```

profile of v0, /device:TPU:64, one launch (start us, length us, event | category | flops | bytes accessed | tf_op | source)
XLA Modules:
  0.0 232.4 jit_solution(3354113923606738813)
XLA Ops:
  7.2 0.0 copy-start
  7.2 0.0 copy-start.5
  7.2 0.0 copy-start.3
  7.2 0.0 all-gather.4.cloned.1.call-start
  7.2 1.5 pad_maximum_fusion.2
  8.7 0.0 all-gather.4.cloned.1.call-update
  8.8 0.0 copy-start.7
  8.8 0.0 copy-start.4
  8.8 0.0 copy-start.6
  8.8 0.0 copy-start.8
  8.8 0.0 all-gather.6.cloned.1.call-start
  8.9 2.7 %copy.33 = bf16[3,2560,128]{1,2,0:T(8,128)(2,1)S(1)} copy(bf16[3,2560,128]{2,1,0:T(8,128)(2,1)} %param.13) | data formatting | bytes 3932160 | tf_op args[3]
  11.5 65.3 %all-gather.4.cloned.1.call-done = bf16[2,128,2560]{2,1,0:T(8,128)(2,1)} async-done(((bf16[2,8,2560]{2,1,0:T(8,128)(2,1)}), bf16[2,128,2560]{2,1,0:T(8,128)(2,1)}) %all-gather.4.cloned.1.call-update) | async-done | bytes 1310736 | tf_op jit(solution)/shard_map/all_gather | solution.py:89
  76.8 1.7 fusion.29
  78.6 0.1 copy.37
  78.8 0.0 copy-done.5
  78.8 0.1 fusion.64
  78.9 0.1 copy.36
  79.0 0.0 copy-done.3
  79.0 15.3 %all-gather = bf16[16,128,128]{2,1,0:T(8,128)(2,1)} all-gather(bf16[4,128,128]{2,1,0:T(8,128)(2,1)S(1)} %pad_maximum_fusion.1), channel_id=2, replica_groups=mesh['y'=8,'zl'=4,'zh'=2,'x'=4,'c'=2] {'zl'}, dimensions={0}, use_global_device_ids=true | all-gather | bytes 655360 | tf_op jit(solution)/shard_map/all_gather | solution.py:69
  94.4 0.0 all-gather.6.cloned.1.call-update
  94.4 0.1 mul.187
  94.5 0.0 copy-done.7
  94.5 0.1 mul.181
  94.6 0.0 copy-done.4
  94.6 0.1 copy.34
  94.7 0.0 copy-done.6
  94.7 0.1 iota_compare_fusion.1
  94.7 0.2 convert_reduce_fusion
  95.0 0.0 copy-done.8
  95.0 0.2 fusion.45
  95.2 0.2 convolution_compare_fusion
  95.4 0.6 dynamic_slice.6
  96.0 0.1 broadcast_bitcast_fusion
  96.1 1.7 fusion.28
  98.0 0.9 fusion.68
  98.9 0.7 fusion.31
  99.6 0.9 fusion.67
  100.6 0.7 fusion.32
  101.3 48.8 %all-gather.6.cloned.1.call-done = bf16[32,4,128,128]{3,2,1,0:T(8,128)(2,1)} async-done(((bf16[4,4,128,128]{3,2,1,0:T(8,128)(2,1)}), bf16[32,4,128,128]{3,2,1,0:T(8,128)(2,1)}) %all-gather.6.cloned.1.call-update) | async-done | bytes 4194320 | tf_op jit(solution)/shard_map/all_gather | solution.py:69
  150.1 4.0 %fusion.62 = (bf16[32,1,128,128]{3,2,1,0:T(8,128)(2,1)}, bf16[32,1,128,128]{3,2,1,0:T(8,128)(2,1)S(1)}, bf16[32,1,128,128]{3,2,1,0:T(8,128)(2,1)}, bf16[32,1,128,128]{3,2,1,0:T(8,128)(2,1)}) fusion(bf16[32,4,128,128]{3,2,1,0:T(8,128)(2,1)} %all-gather.6.cloned.1.call-done), kind=kLoop, calls=%fused_computation.107 | loop fusion | bytes 8388608 | tf_op jit(solution)/shard_map/slice | solution.py:121
  154.1 1.9 copy.39
  156.0 1.3 reshape_squeeze.27
  157.3 1.0 copy.43
  158.3 1.3 reshape_squeeze.31
  159.6 1.9 copy.42
  161.5 0.5 reshape_squeeze.30
  162.0 2.7 %copy.38 = bf16[32,1,128,128]{2,0,3,1:T(8,128)(2,1)} copy(bf16[32,1,128,128]{3,2,1,0:T(8,128)(2,1)} %get-tuple-element.13) | data formatting | bytes 2097152 | tf_op jit(solution)/shard_map/slice | solution.py:121
  164.7 1.7 reshape_squeeze.26
  166.4 0.9 fusion.66
  167.3 0.9 fusion.65
  168.3 1.6 fusion.4
  170.0 0.0 copy-done.2
  170.0 3.1 %fusion.24 = f32[128,2,64]{0,2,1:T(8,128)S(1)} fusion(bf16[4096,2,64]{0,2,1:T(8,128)(2,1)S(1)} %copy-done.2, f32[2,128,4096]{2,1,0:T(8,128)S(1)} %get-tuple-element.23, f32[2,128]{1,0:T(2,128)S(1)} %get-tuple-element.22, pred[4096]{0:T(1024)(128)(4,1)S(1)} %broadcast_bitcast_fusion, f32[128,2]{0,1:T(2,128)S(1)} %get-tuple-element.29), kind=kOutput, calls=%fused_computation.35 | convolution fusion | flops 807419904 | bytes 5314560 | tf_op jit(solution)/shard_map/hqk,khd->qhd/dot_general | solution.py:53
  173.1 0.0 copy-done.1
  173.1 3.1 %fusion.25 = f32[128,2,64]{0,2,1:T(8,128)S(1)} fusion(bf16[4096,2,64]{0,2,1:T(8,128)(2,1)S(1)} %copy-done.1, f32[2,128,4096]{2,1,0:T(8,128)S(1)} %get-tuple-element.21, f32[2,128]{1,0:T(2,128)S(1)} %get-tuple-element.20, pred[4096]{0:T(1024)(128)(4,1)S(1)} %broadcast_bitcast_fusion, f32[128,2]{0,1:T(2,128)S(1)} %get-tuple-element.9), kind=kOutput, calls=%fused_computation.36 | convolution fusion | flops 807419904 | bytes 5314560 | tf_op jit(solution)/shard_map/hqk,khd->qhd/dot_general | solution.py:53
  176.2 0.9 fusion.26
  177.1 0.4 fusion.3
  177.4 0.9 fusion.27
  178.3 0.3 fusion.2
  178.6 0.1 pad_maximum_fusion
  178.8 46.0 %all_to_all.5 = bf16[2,16,8,2560]{3,2,0,1:T(8,128)(2,1)S(1)} all-to-all(bf16[2,16,8,2560]{3,2,0,1:T(8,128)(2,1)S(1)} %pad_maximum_fusion), channel_id=1, replica_groups=mesh['y'=8,'zl'=4,'zh'=2,'x'=4,'c'=2] {'zh','x','c'}, dimensions={1} | all-to-all | bytes 2621440 | tf_op jit(solution)/shard_map/all_to_all | solution.py:124
  224.8 0.2 reduce_sum.114
  225.0 0.6 slice_bitcast_fusion.4
  (18 shorter events, 0.2 us)
Async XLA Ops:
  7.2 169.9 %copy-start = (bf16[128,2560]{1,0:T(8,128)(2,1)S(1)}, bf16[128,2560]{1,0:T(8,128)(2,1)}, u32[]{:S(2)}) copy-start(bf16[128,2560]{1,0:T(8,128)(2,1)} %param.14) | copy-start | bytes 1966084
  7.2 71.6 %copy-start.5 = (f32[128]{0:T(128)S(1)}, f32[128]{0:T(128)}, u32[]{:S(2)}) copy-start(f32[128]{0:T(128)} %param.16) | copy-start | bytes 1540
  7.2 71.8 %copy-start.3 = (bf16[2,128,128]{2,1,0:T(8,128)(2,1)S(1)}, bf16[2,128,128]{2,1,0:T(8,128)(2,1)}, u32[]{:S(2)}) copy-start(bf16[2,128,128]{2,1,0:T(8,128)(2,1)} %param.12) | copy-start | bytes 196612
  7.2 69.6 %all-gather.4.cloned.1.call-start = ((), (), s32[]{:S(2)}) async-start(), calls=%async_computation.1 | async-start | bytes 1392640 | tf_op jit(solution)/shard_map/all_gather | solution.py:89
  8.8 85.7 %copy-start.7 = (f32[128]{0:T(128)S(1)}, f32[128]{0:T(128)}, u32[]{:S(2)}) copy-start(f32[128]{0:T(128)} %param.15) | copy-start | bytes 1540
  8.8 85.8 %copy-start.4 = (s32[32,16]{0,1:T(8,128)S(1)}, s32[32,16]{0,1:T(8,128)}, u32[]{:S(2)}) copy-start(s32[32,16]{0,1:T(8,128)} %param.17) | copy-start | bytes 6148
  8.8 85.9 %copy-start.6 = (s32[32]{0:T(128)S(1)}, s32[32]{0:T(128)}, u32[]{:S(2)}) copy-start(s32[32]{0:T(128)} %param.18) | copy-start | bytes 388
  8.8 86.2 %copy-start.8 = (s32[32]{0:T(128)S(1)}, s32[32]{0:T(128)}, u32[]{:S(2)}) copy-start(s32[32]{0:T(128)} %param.19) | copy-start | bytes 388
  8.8 141.3 %all-gather.6.cloned.1.call-start = ((), (), s32[]{:S(2)}) async-start(), calls=%async_computation.2 | async-start | bytes 4718592 | tf_op jit(solution)/shard_map/all_gather | solution.py:69
  168.3 1.7 copy-start.2
  169.9 3.1 %copy-start.1 = (bf16[4096,2,64]{0,2,1:T(8,128)(2,1)S(1)}, bf16[4096,2,64]{0,2,1:T(8,128)(2,1)}, u32[]{:S(2)}) copy-start(bf16[4096,2,64]{0,2,1:T(8,128)(2,1)} %reshape_squeeze.31) | copy-start | bytes 3145732
Sparse Core Ops, SparseCore 0:
  11.4 65.4 all-gather.3
  94.5 55.5 all-gather.5
where the time goes:
time: 233 us; the launch traced here: 232 us
  waiting for transfers between devices  114 us (49%)
  blocking collectives  61.4 us (26%)
  local copies, waits for them, and re-layouts  20.8 us (9%)
  matrix products  16.3 us (7%)
  between operations  14.4 us (6%)
  other arithmetic  5.38 us (2%)
    all_gather x1, waiting for transfers between devices, on_device(): xs = lax.all_gather(jnp.stack([x_first, x_second]), SEQ, axis=1, tiled=True)  65.3 us
    all_gather x1, waiting for transfers between devices, gather_pipe(): piece = lax.all_gather(piece, name, axis=0, tiled=True)  48.8 us
    all_to_all x1, blocking collectives, on_device(): lax.all_to_all(parts.reshape(2, n_seq, tokens // n_seq, -1), SEQ, 1, 1, t...  46 us
    all_gather x1, blocking collectives, gather_pipe(): piece = lax.all_gather(piece, name, axis=0, tiled=True)  15.3 us
    slice x3, local copies, waits for them, and re-layouts, on_device(): part1 = attend(q1, k1, v1, gathered[:, 0], gathered[:, 1])  8.57 us
    dot_general x4, matrix products, partial_attend(): jnp.einsum('hqk,khd->qhd', weights, values.astype(jnp.float32), precision...  7.93 us
  transfers between devices with their start and end apart: 2, of which 2 were waited for; matrix products, arithmetic and copies ran while one was open for 4% of the time, Pallas kernels for 0%

commit v1 on v0

--- a/solution.py
+++ b/solution.py
@@ -86,7 +86,11 @@
     mine = lax.dynamic_slice_in_dim(linked, me * BPM, BPM, 0)
     own = lax.dynamic_slice_in_dim(mine, me * BPM, BPM, 1)
     remote = mine & (batch_of != me)[None, :]
-    xs = lax.all_gather(jnp.stack([x_first, x_second]), SEQ, axis=1, tiled=True)
+    xin = jnp.stack([x_first, x_second])
+    pages = []
+    for _ in range(lax.axis_size(SEQ)):
+        pages.append(xin)
+    xs = jnp.concatenate(lax.all_to_all(jnp.stack(pages), SEQ, 0, 0), axis=1)
 
     def project(x):
         raw = jnp.einsum("rd,cdh->crh", x, w_qkv, preferred_element_type=jnp.float32)

time: 233 us -> 214 us (0.918)
  waiting for transfers between devices: 114 us -> 84 us
  starting transfers between devices: 0.08 us -> 12 us
    all_gather x1 -> x0, waiting for transfers between devices: 65.3 us -> none  [on_device(): xs = lax.all_gather(jnp.stack([x_first, x_second]), SEQ, axis=1, tiled=True)]
    all_to_all x0 -> x1, waiting for transfers between devices: none -> 34.5 us  [on_device(): xs = jnp.concatenate(lax.all_to_all(jnp.stack(pages), SEQ, 0, 0), axis=1)]
    all_to_all x0 -> x1, starting transfers between devices: none -> 12 us  [on_device(): xs = jnp.concatenate(lax.all_to_all(jnp.stack(pages), SEQ, 0, 0), axis=1)]
where the time goes in v1:
time: 214 us; the launch traced here: 213 us
  waiting for transfers between devices  84 us (39%)
  blocking collectives  59.7 us (28%)
  local copies, waits for them, and re-layouts  21.9 us (10%)
  matrix products  16.3 us (8%)
  between operations  14.4 us (7%)
  starting transfers between devices  12 us (6%)
  other arithmetic  4.77 us (2%)
    all_gather x1, waiting for transfers between devices, gather_pipe(): piece = lax.all_gather(piece, name, axis=0, tiled=True)  49.5 us
    all_to_all x1, blocking collectives, on_device(): lax.all_to_all(parts.reshape(2, n_seq, tokens // n_seq, -1), SEQ, 1, 1, t...  46 us
    all_to_all x1, waiting for transfers between devices, on_device(): xs = jnp.concatenate(lax.all_to_all(jnp.stack(pages), SEQ, 0, 0), axis=1)  34.5 us
    all_gather x1, blocking collectives, gather_pipe(): piece = lax.all_gather(piece, name, axis=0, tiled=True)  13.7 us
    all_to_all x1, starting transfers between devices, on_device(): xs = jnp.concatenate(lax.all_to_all(jnp.stack(pages), SEQ, 0, 0), axis=1)  12 us
    slice x3, local copies, waits for them, and re-layouts, on_device(): part1 = attend(q1, k1, v1, gathered[:, 0], gathered[:, 1])  8.57 us
    dot_general x4, matrix products, partial_attend(): jnp.einsum('hqk,khd->qhd', weights, values.astype(jnp.float32), precision...  7.93 us
  transfers between devices with their start and end apart: 2, of which 2 were waited for; matrix products, arithmetic and copies ran while one was open for 4% of the time, Pallas kernels for 0%

profile of v1, /device:TPU:64, one launch (start us, length us, event | category | flops | bytes accessed | tf_op | source)
XLA Modules:
  0.0 213.2 jit_solution(6781140944320013016)
XLA Ops:
  7.2 0.0 copy-start
  7.2 0.9 pad_maximum_fusion.2
  8.1 1.2 stack.20
  9.2 12.0 %all-to-all-start = ((bf16[16,2,8,2560]{3,2,1,0:T(8,128)(2,1)}), bf16[16,2,8,2560]{3,2,1,0:T(8,128)(2,1)}, u32[]{:S(2)}, u32[]{:S(2)}) async-start(bf16[16,2,8,2560]{3,2,1,0:T(8,128)(2,1)} %stack.20), calls=%async_computation | async-start | bytes 2621440 | tf_op jit(solution)/shard_map/all_to_all | solution.py:93
  21.2 0.0 copy-start.5
  21.3 0.0 copy-start.3
  21.3 0.0 copy-start.7
  21.3 0.0 copy-start.4
  21.3 0.0 copy-start.6
  21.3 0.0 copy-start.8
  21.3 0.0 all-gather.3.cloned.1.call-start
  21.4 2.7 %copy.33 = bf16[3,2560,128]{1,2,0:T(8,128)(2,1)S(1)} copy(bf16[3,2560,128]{2,1,0:T(8,128)(2,1)} %param.13) | data formatting | bytes 3932160 | tf_op args[3]
  24.1 34.5 %all-to-all-done = bf16[16,2,8,2560]{3,2,1,0:T(8,128)(2,1)} async-done(((bf16[16,2,8,2560]{3,2,1,0:T(8,128)(2,1)}), bf16[16,2,8,2560]{3,2,1,0:T(8,128)(2,1)}, u32[]{:S(2)}, u32[]{:S(2)}) %all-to-all-start) | async-done | bytes 1310752 | tf_op jit(solution)/shard_map/all_to_all | solution.py:93
  58.5 1.7 fusion.29
  60.3 0.1 copy.37
  60.5 0.0 copy-done.5
  60.5 0.1 fusion.64
  60.6 0.1 copy.36
  60.7 0.0 copy-done.3
  60.7 13.7 %all-gather = bf16[16,128,128]{2,1,0:T(8,128)(2,1)} all-gather(bf16[4,128,128]{2,1,0:T(8,128)(2,1)S(1)} %pad_maximum_fusion.1), channel_id=2, replica_groups=mesh['y'=8,'zl'=4,'zh'=2,'x'=4,'c'=2] {'zl'}, dimensions={0}, use_global_device_ids=true | all-gather | bytes 655360 | tf_op jit(solution)/shard_map/all_gather | solution.py:69
  74.4 0.0 all-gather.3.cloned.1.call-update
  74.5 0.1 mul.187
  74.6 0.0 copy-done.7
  74.6 0.1 mul.181
  74.6 0.0 copy-done.4
  74.6 0.1 copy.34
  74.7 0.0 copy-done.6
  74.7 0.1 iota_compare_fusion.1
  74.8 0.2 convert_reduce_fusion
  75.0 0.0 copy-done.8
  75.0 0.2 fusion.45
  75.2 0.2 convolution_compare_fusion
  75.4 0.6 dynamic_slice.6
  76.1 0.1 broadcast_bitcast_fusion
  76.1 1.7 fusion.28
  78.0 0.9 fusion.68
  79.0 0.7 fusion.31
  79.7 0.9 fusion.67
  80.6 0.7 fusion.32
  81.3 49.5 %all-gather.3.cloned.1.call-done = bf16[32,4,128,128]{3,2,1,0:T(8,128)(2,1)} async-done(((bf16[4,4,128,128]{3,2,1,0:T(8,128)(2,1)}), bf16[32,4,128,128]{3,2,1,0:T(8,128)(2,1)}) %all-gather.3.cloned.1.call-update) | async-done | bytes 4194320 | tf_op jit(solution)/shard_map/all_gather | solution.py:69
  130.8 4.0 %fusion.62 = (bf16[32,1,128,128]{3,2,1,0:T(8,128)(2,1)}, bf16[32,1,128,128]{3,2,1,0:T(8,128)(2,1)S(1)}, bf16[32,1,128,128]{3,2,1,0:T(8,128)(2,1)}, bf16[32,1,128,128]{3,2,1,0:T(8,128)(2,1)}) fusion(bf16[32,4,128,128]{3,2,1,0:T(8,128)(2,1)} %all-gather.3.cloned.1.call-done), kind=kLoop, calls=%fused_computation.107 | loop fusion | bytes 8388608 | tf_op jit(solution)/shard_map/slice | solution.py:125
  134.8 1.9 copy.39
  136.7 1.3 reshape_squeeze.27
  138.0 1.0 copy.43
  139.0 1.3 reshape_squeeze.31
  140.3 1.9 copy.42
  142.2 0.5 reshape_squeeze.30
  142.7 2.7 %copy.38 = bf16[32,1,128,128]{2,0,3,1:T(8,128)(2,1)} copy(bf16[32,1,128,128]{3,2,1,0:T(8,128)(2,1)} %get-tuple-element.13) | data formatting | bytes 2097152 | tf_op jit(solution)/shard_map/slice | solution.py:125
  145.4 1.7 reshape_squeeze.26
  147.1 0.9 fusion.66
  148.0 0.9 fusion.65
  149.0 1.6 fusion.4
  150.7 0.0 copy-done.2
  150.7 3.1 %fusion.24 = f32[128,2,64]{0,2,1:T(8,128)S(1)} fusion(bf16[4096,2,64]{0,2,1:T(8,128)(2,1)S(1)} %copy-done.2, f32[2,128,4096]{2,1,0:T(8,128)S(1)} %get-tuple-element.23, f32[2,128]{1,0:T(2,128)S(1)} %get-tuple-element.22, pred[4096]{0:T(1024)(128)(4,1)S(1)} %broadcast_bitcast_fusion, f32[128,2]{0,1:T(2,128)S(1)} %get-tuple-element.29), kind=kOutput, calls=%fused_computation.35 | convolution fusion | flops 807419904 | bytes 5314560 | tf_op jit(solution)/shard_map/hqk,khd->qhd/dot_general | solution.py:53
  153.8 0.0 copy-done.1
  153.8 3.1 %fusion.25 = f32[128,2,64]{0,2,1:T(8,128)S(1)} fusion(bf16[4096,2,64]{0,2,1:T(8,128)(2,1)S(1)} %copy-done.1, f32[2,128,4096]{2,1,0:T(8,128)S(1)} %get-tuple-element.21, f32[2,128]{1,0:T(2,128)S(1)} %get-tuple-element.20, pred[4096]{0:T(1024)(128)(4,1)S(1)} %broadcast_bitcast_fusion, f32[128,2]{0,1:T(2,128)S(1)} %get-tuple-element.9), kind=kOutput, calls=%fused_computation.36 | convolution fusion | flops 807419904 | bytes 5314560 | tf_op jit(solution)/shard_map/hqk,khd->qhd/dot_general | solution.py:53
  156.9 0.9 fusion.26
  157.8 0.4 fusion.3
  158.1 0.9 fusion.27
  159.0 0.3 fusion.2
  159.4 0.1 pad_maximum_fusion
  159.5 46.0 %all_to_all.10 = bf16[2,16,8,2560]{3,2,0,1:T(8,128)(2,1)S(1)} all-to-all(bf16[2,16,8,2560]{3,2,0,1:T(8,128)(2,1)S(1)} %pad_maximum_fusion), channel_id=1, replica_groups=mesh['y'=8,'zl'=4,'zh'=2,'x'=4,'c'=2] {'zh','x','c'}, dimensions={1} | all-to-all | bytes 2621440 | tf_op jit(solution)/shard_map/all_to_all | solution.py:128
  205.5 0.2 reduce_sum.114
  205.7 0.6 slice_bitcast_fusion.4
  (18 shorter events, 0.2 us)
Async XLA Ops:
  7.2 150.6 %copy-start = (bf16[128,2560]{1,0:T(8,128)(2,1)S(1)}, bf16[128,2560]{1,0:T(8,128)(2,1)}, u32[]{:S(2)}) copy-start(bf16[128,2560]{1,0:T(8,128)(2,1)} %param.14) | copy-start | bytes 1966084
  9.2 49.3 %all-to-all-start = ((bf16[16,2,8,2560]{3,2,1,0:T(8,128)(2,1)}), bf16[16,2,8,2560]{3,2,1,0:T(8,128)(2,1)}, u32[]{:S(2)}, u32[]{:S(2)}) async-start(bf16[16,2,8,2560]{3,2,1,0:T(8,128)(2,1)} %stack.20), calls=%async_computation | async-start | bytes 2621440 | tf_op jit(solution)/shard_map/all_to_all | solution.py:93
  21.2 39.2 %copy-start.5 = (f32[128]{0:T(128)S(1)}, f32[128]{0:T(128)}, u32[]{:S(2)}) copy-start(f32[128]{0:T(128)} %param.16) | copy-start | bytes 1540
  21.3 39.4 %copy-start.3 = (bf16[2,128,128]{2,1,0:T(8,128)(2,1)S(1)}, bf16[2,128,128]{2,1,0:T(8,128)(2,1)}, u32[]{:S(2)}) copy-start(bf16[2,128,128]{2,1,0:T(8,128)(2,1)} %param.12) | copy-start | bytes 196612
  21.3 53.3 %copy-start.7 = (f32[128]{0:T(128)S(1)}, f32[128]{0:T(128)}, u32[]{:S(2)}) copy-start(f32[128]{0:T(128)} %param.15) | copy-start | bytes 1540
  21.3 53.4 %copy-start.4 = (s32[32,16]{0,1:T(8,128)S(1)}, s32[32,16]{0,1:T(8,128)}, u32[]{:S(2)}) copy-start(s32[32,16]{0,1:T(8,128)} %param.17) | copy-start | bytes 6148
  21.3 53.4 %copy-start.6 = (s32[32]{0:T(128)S(1)}, s32[32]{0:T(128)}, u32[]{:S(2)}) copy-start(s32[32]{0:T(128)} %param.18) | copy-start | bytes 388
  21.3 53.7 %copy-start.8 = (s32[32]{0:T(128)S(1)}, s32[32]{0:T(128)}, u32[]{:S(2)}) copy-start(s32[32]{0:T(128)} %param.19) | copy-start | bytes 388
  21.3 109.5 %all-gather.3.cloned.1.call-start = ((), (), s32[]{:S(2)}) async-start(), calls=%async_computation.2 | async-start | bytes 4718592 | tf_op jit(solution)/shard_map/all_gather | solution.py:69
  149.0 1.7 copy-start.2
  150.6 3.1 %copy-start.1 = (bf16[4096,2,64]{0,2,1:T(8,128)(2,1)S(1)}, bf16[4096,2,64]{0,2,1:T(8,128)(2,1)}, u32[]{:S(2)}) copy-start(bf16[4096,2,64]{0,2,1:T(8,128)(2,1)} %reshape_squeeze.31) | copy-start | bytes 3145732
Sparse Core Ops, SparseCore 0:
  74.6 56.1 all-gather.2
